TPU v7x, 256 devices: a whole 4x4x8 slice. The times are simulated.
256 devices in a mesh: gx: 64 (over z, y, core), gy: 4 (over x).
Axes of the slice: x: 4, y: 4, z: 8, core: 2. Of those that a mesh axis runs over, the one named last changes fastest.
Arguments:
- embeds: bfloat16 [256, 2048, 768], P('gx', 'gy'), may hold values from -6 to 6
- fetch_list: int32 [2, 64, 64], replicated, may hold values from 0 to 16383, as said below
- partners: int32 [2, 64, 64, 2], replicated, may hold values from 0 to 255, as said below
- counts: int32 [256], replicated, may hold values from 512 to 2048
Outputs:
- nearest: float32 [256, 2048], P('gx', 'gy')
Inputs may be any that keep to these rules, and one draw needn't show every extreme that they name: fetch_list[w, h, g] // 64 is a block stored by index g of gx, that is g * 4 <= fetch_list[w, h, g] // 64 < (g + 1) * 4. partners[w, h, g, :] are 2 different blocks stored by index h of gx, none equal to fetch_list[w, h, g] // 64.
All inputs are finite; a program needn't handle non-finite values.
Results may differ from a plain program's by a relative error of at most 0.0003.
Values may be sent and summed in bfloat16 or wider, within the bound.
No kernel may reach another device: no remote copies, remote signals or barrier semaphores. Data moves between devices by JAX's collectives and lax.ppermute only.
A program may use at most 192 MiB of HBM per device.

v0:
```python
import jax
import jax.numpy as jnp
from jax import lax
from jax.sharding import PartitionSpec as P

SLICE = 8
EPS = 1e-06


def normalize(source):
    values = source.astype(jnp.float32)
    return (values * lax.rsqrt(jnp.sum(values * values, axis=-1, keepdims=True) + EPS)).astype(
        jnp.bfloat16
    )


def dense_tiles(arrived, row_valid, chosen, owned_full, col_valid):
    slots, lent_rows, width = arrived.shape
    owned, block, _ = owned_full.shape
    flat_rows = arrived.reshape(slots * lent_rows, width)
    listed = jnp.any(
        chosen[:, :, None] == jnp.arange(owned, dtype=jnp.int32)[None, None, :], axis=1
    )
    listed_pairs = jnp.transpose(listed.reshape(slots, owned // 2, 2), (1, 0, 2))
    column_pairs = owned_full.reshape(owned // 2, 2, block, width)
    valid_pairs = col_valid.reshape(owned // 2, 2, block)

    def advance(best_rows, entries):
        columns, picked, valid_cols = entries
        scores = jnp.einsum("rd,cbd->rcb", flat_rows, columns, preferred_element_type=jnp.float32)
        scores = scores.reshape(slots, lent_rows, 2, block)
        keep = row_valid[:, :, None, None] & picked[:, None, :, None] & valid_cols[None, None, :, :]
        scores = jnp.where(keep, scores, jnp.float32(-1.0))
        return (jnp.maximum(best_rows, jnp.max(scores, axis=(2, 3))), jnp.max(scores, axis=(0, 1)))

    start = jnp.full((slots, lent_rows), -1.0, jnp.float32)
    best_rows, col_parts = lax.scan(advance, start, (column_pairs, listed_pairs, valid_pairs))
    return (best_rows, col_parts.reshape(owned, block))


def on_device(embeds, fetch_list, partners, counts):
    owned, quarter, width = embeds.shape
    slice_rows = SLICE
    pieces = quarter // slice_rows
    my_group = lax.axis_index("gx")
    my_lane = lax.axis_index("gy")
    block = quarter * lax.axis_size("gy")
    first = my_group * owned
    waves = fetch_list.shape[0]
    own_unit = normalize(embeds)
    own_pieces = own_unit.reshape(owned, pieces, slice_rows, width)
    owned_full = lax.all_gather(own_unit, "gy", axis=1, tiled=True)
    positions = jnp.arange(block, dtype=jnp.int32)
    own_counts = lax.dynamic_slice_in_dim(counts, first, owned)
    col_valid = positions[None, :] < own_counts[:, None]
    row_positions = my_lane * quarter + jnp.arange(quarter, dtype=jnp.int32)
    slice_offsets = my_lane * quarter + jnp.arange(slice_rows, dtype=jnp.int32)
    local_ids = jnp.arange(owned, dtype=jnp.int32)
    piece_ids = jnp.arange(pieces, dtype=jnp.int32)
    row_total = jnp.full((owned, quarter), -1.0, jnp.float32)
    col_total = jnp.full((owned, block), -1.0, jnp.float32)
    for wave_index in range(waves):
        tiles = lax.dynamic_index_in_dim(fetch_list[wave_index], my_group, 1, False)
        outgoing_sent_block = tiles // pieces - first
        outgoing_sent_piece = tiles % pieces
        outbound = own_pieces[outgoing_sent_block, outgoing_sent_piece]
        arrived = lax.all_to_all(outbound, "gx", split_axis=0, concat_axis=0, tiled=True)
        incoming = lax.dynamic_index_in_dim(fetch_list[wave_index], my_group, 0, False)
        arrived_counts = counts[incoming // pieces]
        arrived_rows = (incoming % pieces)[:, None] * slice_rows + slice_offsets[None, :]
        row_valid = arrived_rows < arrived_counts[:, None]
        chosen = lax.dynamic_index_in_dim(partners[wave_index], my_group, 0, False) - first
        row_best, col_best = dense_tiles(arrived, row_valid, chosen, owned_full, col_valid)
        returned = lax.all_to_all(row_best, "gx", split_axis=0, concat_axis=0, tiled=True)
        match = (outgoing_sent_block[:, None, None] == local_ids[None, :, None]) & (
            outgoing_sent_piece[:, None, None] == piece_ids[None, None, :]
        )
        placed = jnp.max(
            jnp.where(match[:, :, :, None], returned[:, None, None, :], jnp.float32(-1.0)), axis=0
        )
        row_total = jnp.maximum(row_total, placed.reshape(owned, quarter))
        col_total = jnp.maximum(col_total, col_best)
    col_all = lax.pmax(col_total, "gy")
    col_mine = lax.dynamic_slice_in_dim(col_all, my_lane * quarter, quarter, 1)
    nearest = jnp.maximum(row_total, col_mine)
    mine_valid = row_positions[None, :] < own_counts[:, None]
    return jnp.where(mine_valid, nearest, jnp.float32(-1.0))


def solution(mesh):
    in_specs = (P("gx", "gy", None), P(), P(), P())
    out_specs = P("gx", "gy")
    return jax.shard_map(
        on_device, mesh=mesh, in_specs=in_specs, out_specs=out_specs, check_vma=False
    )
```

profile of v0, /device:TPU:1, one launch (start us, length us, event | category | flops | bytes accessed | tf_op | source)
XLA Modules:
  0.0 224.2 jit_solution(3750707437659595756)
XLA Ops:
  6.5 2.7 %fusion.18 = f32[4,512]{1,0:T(4,128)S(1)} fusion(bf16[4,512,768]{2,1,0:T(8,128)(2,1)} %param.8), kind=kLoop, calls=%fused_computation.36 | loop fusion | flops 4716544 | bytes 3153920 | tf_op jit(solution)/shard_map/reduce_sum | solution.py:12
  9.3 4.1 %fusion.19 = bf16[4,512,768]{2,1,0:T(8,128)(2,1)} fusion(bf16[4,512,768]{2,1,0:T(8,128)(2,1)} %param.8, f32[4,512]{1,0:T(4,128)S(1)} %add_rsqrt_fusion), kind=kLoop, calls=%fused_computation.37 | loop fusion | flops 4718592 | bytes 6299648 | tf_op jit(solution)/shard_map/convert_element_type | solution.py:12
  13.4 0.0 all-gather.2.cloned.1.call-update
  13.5 0.2 dynamic-slice_reduce_fusion
  13.7 2.2 %fusion.48 = bf16[4,64,8,768]{3,2,1,0:T(8,128)(2,1)} fusion(f32[4,512]{1,0:T(4,128)S(1)} %add_rsqrt_fusion, bf16[4,512,768]{2,1,0:T(8,128)(2,1)S(1)} %copy-done.1), kind=kLoop, calls=%fused_computation.135 | loop fusion | flops 4718592 | bytes 6299648 | tf_op jit(solution)/shard_map/reshape | solution.py:51
  16.0 3.5 %gather_fusion.3 = bf16[64,8,768]{2,1,0:T(8,128)(2,1)} fusion(bf16[4,64,8,768]{3,2,1,0:T(8,128)(2,1)} %fusion.48, s32[64]{0:T(128)S(1)} %fusion.42), kind=kCustom, calls=%fused_computation.3 | custom fusion | bytes 1573376 | tf_op jit(solution)/shard_map/gather | solution.py:66
  19.4 13.1 %all-to-all-start.2 = ((bf16[64,8,768]{2,1,0:T(8,128)(2,1)}), bf16[64,8,768]{2,1,0:T(8,128)(2,1)S(1)}, u32[]{:S(2)}, u32[]{:S(2)}) async-start(bf16[64,8,768]{2,1,0:T(8,128)(2,1)} %gather_fusion.3), calls=%async_computation.2 | async-start | bytes 1572864 | tf_op jit(solution)/shard_map/all_to_all | solution.py:67
  32.7 0.1 dynamic_slice.48
  32.8 0.1 lt.161
  32.9 0.8 gather_fusion.2
  33.7 0.2 dynamic-slice_reduce_fusion.1
  33.9 3.7 %gather_fusion.1 = bf16[64,8,768]{2,1,0:T(8,128)(2,1)} fusion(bf16[4,64,8,768]{3,2,1,0:T(8,128)(2,1)} %fusion.48, s32[64]{0:T(128)S(1)} %fusion.43), kind=kCustom, calls=%fused_computation.1 | custom fusion | bytes 1573376 | tf_op jit(solution)/shard_map/gather | solution.py:66
  37.7 0.8 gather_fusion
  38.5 0.1 iota_compare_fusion
  38.6 0.1 iota_compare_fusion.1
  38.7 0.1 iota_compare_fusion.3
  38.8 0.1 iota_compare_fusion.4
  38.8 0.1 broadcast_and_fusion.2
  39.0 0.1 broadcast_and_fusion.3
  39.1 0.1 iota_compare_fusion.2
  39.2 16.4 %all-to-all-done.2 = bf16[64,8,768]{2,1,0:T(8,128)(2,1)S(1)} async-done(((bf16[64,8,768]{2,1,0:T(8,128)(2,1)}), bf16[64,8,768]{2,1,0:T(8,128)(2,1)S(1)}, u32[]{:S(2)}, u32[]{:S(2)}) %all-to-all-start.2) | async-done | bytes 786464 | tf_op jit(solution)/shard_map/all_to_all | solution.py:67
  55.6 5.9 %all-to-all-start = ((bf16[64,8,768]{2,1,0:T(8,128)(2,1)}), bf16[64,8,768]{2,1,0:T(8,128)(2,1)S(1)}, u32[]{:S(2)}, u32[]{:S(2)}) async-start(bf16[64,8,768]{2,1,0:T(8,128)(2,1)} %gather_fusion.1), calls=%async_computation | async-start | bytes 1572864 | tf_op jit(solution)/shard_map/all_to_all | solution.py:67
  61.5 76.8 %all-gather.2.cloned.1.call-done = bf16[4,2048,768]{2,1,0:T(8,128)(2,1)} async-done(((bf16[4,512,768]{2,1,0:T(8,128)(2,1)}), bf16[4,2048,768]{2,1,0:T(8,128)(2,1)}) %all-gather.2.cloned.1.call-update) | async-done | bytes 12582928 | tf_op jit(solution)/shard_map/all_gather | solution.py:52
  138.3 15.5 %while.27 = (s32[]{:T(128)}, f32[64,8]{1,0:T(8,128)}, f32[2,2,2048]{2,1,0:T(2,128)S(1)}, pred[2,64,2]{1,2,0:T(4,128)(4,1)S(1)}, pred[2,2,2048]{2,1,0:T(4,128)(4,...) while((s32[]{:T(128)}, f32[64,8]{1,0:T(8,128)}, ...), condition=%wide.region_11.12_spmd.clone, body=%wide.region_8.11_spmd.clone.sunk | while | flops 3229612544 | bytes 7160887 | solution.py:37
  138.4 0.1 and.439
  138.5 0.1 and.440
  138.6 0.1 add_compare_fusion.5
  138.7 0.1 and.441
  138.8 6.2 %fusion.52 = (f32[2,2048]{1,0:T(2,128)S(1)}, f32[512]{0:T(512)S(1)}) fusion(pred[2,2048]{1,0:T(4,128)(4,1)S(1)} %dynamic-slice_bitcast_fusion.10, pred[512,2]{0,1:T(4,128)(4,1)S(1)} %broadcast_and_fusion.7, bf16[512,768]{1,0:T(8,128)(2,1)S(1)} %get-tuple-element.389, bf16[2,2,2048,768]{3,2,1,0:T(8,128)(2,1)} %get-tuple-element.388, s32[]{:T(128)S(6)} %copy.19), kind=kOutput, calls=%fused_computation.21.clone.1 | convolution fusion | flops 3229609472 | bytes 7101444 | tf_op jit(solution)/shard_map/while/body/eval_jaxpr/rd,cbd->rcb/dot_general | solution.py:30
  145.0 0.1 reduce_max.79
  145.1 0.6 select_maximum_fusion.5
  145.8 0.1 and.439
  145.9 0.1 and.440
  146.0 0.1 add_compare_fusion.5
  146.1 0.1 and.441
  146.2 6.2 %fusion.52 = (f32[2,2048]{1,0:T(2,128)S(1)}, f32[512]{0:T(512)S(1)}) fusion(pred[2,2048]{1,0:T(4,128)(4,1)S(1)} %dynamic-slice_bitcast_fusion.10, pred[512,2]{0,1:T(4,128)(4,1)S(1)} %broadcast_and_fusion.7, bf16[512,768]{1,0:T(8,128)(2,1)S(1)} %get-tuple-element.389, bf16[2,2,2048,768]{3,2,1,0:T(8,128)(2,1)} %get-tuple-element.388, s32[]{:T(128)S(6)} %copy.19), kind=kOutput, calls=%fused_computation.21.clone.1 | convolution fusion | flops 3229609472 | bytes 7101444 | tf_op jit(solution)/shard_map/while/body/eval_jaxpr/rd,cbd->rcb/dot_general | solution.py:30
  152.4 0.1 reduce_max.79
  152.5 1.4 select_maximum_fusion.5
  153.9 0.0 all-to-all-done
  153.9 10.9 %all-to-all-start.3 = ((f32[64,1,8]{2,1,0:T(1,128)}), f32[64,1,8]{2,1,0:T(1,128)S(1)}, u32[]{:S(2)}, u32[]{:S(2)}) async-start(f32[64,1,8]{2,1,0:T(1,128)} %bitcast.18), calls=%async_computation.3 | async-start | bytes 65536 | tf_op jit(solution)/shard_map/all_to_all | solution.py:74
  164.8 15.5 %while.26 = (s32[]{:T(128)}, f32[64,8]{1,0:T(8,128)}, f32[2,2,2048]{2,1,0:T(2,128)S(1)}, pred[2,64,2]{1,2,0:T(4,128)(4,1)S(1)}, pred[2,2,2048]{2,1,0:T(4,128)(4,...) while((s32[]{:T(128)}, f32[64,8]{1,0:T(8,128)}, ...), condition=%wide.region_5.6_spmd.clone, body=%wide.region_2.5_spmd.clone.sunk | while | flops 3229612544 | bytes 7160887 | solution.py:37
  164.8 0.1 and.431
  164.9 0.1 and.432
  165.0 0.1 add_compare_fusion.4
  165.1 0.1 and.433
  165.2 6.2 %fusion.51 = (f32[2,2048]{1,0:T(2,128)S(1)}, f32[512]{0:T(512)S(1)}) fusion(pred[2,2048]{1,0:T(4,128)(4,1)S(1)} %dynamic-slice_bitcast_fusion.8, pred[512,2]{0,1:T(4,128)(4,1)S(1)} %broadcast_and_fusion.6, bf16[512,768]{1,0:T(8,128)(2,1)S(1)} %get-tuple-element.425, bf16[2,2,2048,768]{3,2,1,0:T(8,128)(2,1)} %get-tuple-element.424, s32[]{:T(128)S(6)} %copy.28), kind=kOutput, calls=%fused_computation.7.clone.1 | convolution fusion | flops 3229609472 | bytes 7101444 | tf_op jit(solution)/shard_map/while/body/eval_jaxpr/rd,cbd->rcb/dot_general | solution.py:30
  171.4 0.1 reduce_max.77
  171.5 0.6 select_maximum_fusion.4
  172.2 0.1 and.431
  172.3 0.1 and.432
  172.4 0.1 add_compare_fusion.4
  172.5 0.1 and.433
  172.6 6.2 %fusion.51 = (f32[2,2048]{1,0:T(2,128)S(1)}, f32[512]{0:T(512)S(1)}) fusion(pred[2,2048]{1,0:T(4,128)(4,1)S(1)} %dynamic-slice_bitcast_fusion.8, pred[512,2]{0,1:T(4,128)(4,1)S(1)} %broadcast_and_fusion.6, bf16[512,768]{1,0:T(8,128)(2,1)S(1)} %get-tuple-element.425, bf16[2,2,2048,768]{3,2,1,0:T(8,128)(2,1)} %get-tuple-element.424, s32[]{:T(128)S(6)} %copy.28), kind=kOutput, calls=%fused_computation.7.clone.1 | convolution fusion | flops 3229609472 | bytes 7101444 | tf_op jit(solution)/shard_map/while/body/eval_jaxpr/rd,cbd->rcb/dot_general | solution.py:30
  178.8 0.1 reduce_max.77
  178.9 1.4 select_maximum_fusion.4
  180.4 12.3 %pmax.7 = f32[4,2048]{1,0:T(4,128)S(1)} all-reduce(f32[4,2048]{1,0:T(4,128)S(1)} %max.26), channel_id=1, replica_groups=mesh['gx'=64,'gy'=4] {'gy'}, use_global_device_ids=true, to_apply=%region_13.14 | all-reduce | flops 8192 | bytes 65536 | tf_op jit(solution)/shard_map/pmax | solution.py:83
  192.7 0.0 all-to-all-done.3
  192.7 14.1 %all-to-all-start.1 = ((f32[64,1,8]{2,1,0:T(1,128)}), f32[64,1,8]{2,1,0:T(1,128)S(1)}, u32[]{:S(2)}, u32[]{:S(2)}) async-start(f32[64,1,8]{2,1,0:T(1,128)} %bitcast.9), calls=%async_computation.1 | async-start | bytes 65536 | tf_op jit(solution)/shard_map/all_to_all | solution.py:74
  206.8 0.2 select_reduce_fusion
  207.0 9.2 %all-to-all-done.1 = f32[64,1,8]{2,1,0:T(1,128)S(1)} async-done(((f32[64,1,8]{2,1,0:T(1,128)}), f32[64,1,8]{2,1,0:T(1,128)S(1)}, u32[]{:S(2)}, u32[]{:S(2)}) %all-to-all-start.1) | async-done | bytes 2080 | tf_op jit(solution)/shard_map/all_to_all | solution.py:74
  216.2 0.2 select_reduce_fusion.1
  216.4 0.1 copy.13
  216.5 0.1 max.24
  216.6 0.7 maximum_select_fusion
  (50 shorter events, 0.5 us)
Async XLA Ops:
  6.5 7.2 %copy-start.1 = (bf16[4,512,768]{2,1,0:T(8,128)(2,1)S(1)}, bf16[4,512,768]{2,1,0:T(8,128)(2,1)}, u32[]{:S(2)}) copy-start(bf16[4,512,768]{2,1,0:T(8,128)(2,1)} %param.8) | copy-start | bytes 9437188
  6.5 6.9 %copy-start.3 = (s32[2,64,64]{2,1,0:T(8,128)S(1)}, s32[2,64,64]{2,1,0:T(8,128)}, u32[]{:S(2)}) copy-start(s32[2,64,64]{2,1,0:T(8,128)} %param.9) | copy-start | bytes 98308
  6.5 131.8 %all-gather.2.cloned.1.call-start = ((), (), s32[]{:S(2)}) async-start(), calls=%async_computation.4 | async-start | bytes 15728640 | tf_op jit(solution)/shard_map/all_gather | solution.py:52
  13.4 19.2 %copy-start.2 = (s32[2,64,64,2]{2,3,1,0:T(2,128)S(1)}, s32[2,64,64,2]{2,3,1,0:T(2,128)}, u32[]{:S(2)}) copy-start(s32[2,64,64,2]{2,3,1,0:T(2,128)} %param.10) | copy-start | bytes 196612
  13.4 19.2 %copy-start = (s32[256]{0:T(256)S(1)}, s32[256]{0:T(256)}, u32[]{:S(2)}) copy-start(s32[256]{0:T(256)} %param.11) | copy-start | bytes 3076
  19.4 36.2 %all-to-all-start.2 = ((bf16[64,8,768]{2,1,0:T(8,128)(2,1)}), bf16[64,8,768]{2,1,0:T(8,128)(2,1)S(1)}, u32[]{:S(2)}, u32[]{:S(2)}) async-start(bf16[64,8,768]{2,1,0:T(8,128)(2,1)} %gather_fusion.3), calls=%async_computation.2 | async-start | bytes 1572864 | tf_op jit(solution)/shard_map/all_to_all | solution.py:67
  55.6 98.3 %all-to-all-start = ((bf16[64,8,768]{2,1,0:T(8,128)(2,1)}), bf16[64,8,768]{2,1,0:T(8,128)(2,1)S(1)}, u32[]{:S(2)}, u32[]{:S(2)}) async-start(bf16[64,8,768]{2,1,0:T(8,128)(2,1)} %gather_fusion.1), calls=%async_computation | async-start | bytes 1572864 | tf_op jit(solution)/shard_map/all_to_all | solution.py:67
  153.9 38.8 %all-to-all-start.3 = ((f32[64,1,8]{2,1,0:T(1,128)}), f32[64,1,8]{2,1,0:T(1,128)S(1)}, u32[]{:S(2)}, u32[]{:S(2)}) async-start(f32[64,1,8]{2,1,0:T(1,128)} %bitcast.18), calls=%async_computation.3 | async-start | bytes 65536 | tf_op jit(solution)/shard_map/all_to_all | solution.py:74
  192.7 23.5 %all-to-all-start.1 = ((f32[64,1,8]{2,1,0:T(1,128)}), f32[64,1,8]{2,1,0:T(1,128)S(1)}, u32[]{:S(2)}, u32[]{:S(2)}) async-start(f32[64,1,8]{2,1,0:T(1,128)} %bitcast.9), calls=%async_computation.1 | async-start | bytes 65536 | tf_op jit(solution)/shard_map/all_to_all | solution.py:74
Sparse Core Ops, SparseCore 0:
  13.6 124.6 all-gather.1
where the time goes:
time: 225 us; the launch traced here: 224 us
  waiting for transfers between devices  102 us (45%)
  starting transfers between devices  44 us (20%)
  matrix products  24.8 us (11%)
  other arithmetic  15.5 us (7%)
  between operations  13.7 us (6%)
  blocking collectives  12.3 us (5%)
  local copies, waits for them, and re-layouts  11.2 us (5%)
    all_gather x1, waiting for transfers between devices, on_device(): owned_full = lax.all_gather(own_unit, 'gy', axis=1, tiled=True)  76.8 us
    all_to_all x2, starting transfers between devices, on_device(): lax.all_to_all(row_best, 'gx', split_axis=0, concat_axis=0, tiled=True)  24.9 us
    dot_general x4, matrix products, advance(): jnp.einsum('rd,cbd->rcb', flat_rows, columns, preferred_element_type=jnp....  24.8 us
    all_to_all x2, starting transfers between devices, on_device(): lax.all_to_all(outbound, 'gx', split_axis=0, concat_axis=0, tiled=True)  19.1 us
    all_to_all x2, waiting for transfers between devices, on_device(): lax.all_to_all(outbound, 'gx', split_axis=0, concat_axis=0, tiled=True)  16.4 us
    pmax x1, blocking collectives, on_device(): col_all = lax.pmax(col_total, 'gy')  12.3 us
    all_to_all x2, waiting for transfers between devices, on_device(): lax.all_to_all(row_best, 'gx', split_axis=0, concat_axis=0, tiled=True)  9.17 us
    gather x2, local copies, waits for them, and re-layouts, on_device(): outbound = own_pieces[outgoing_sent_block, outgoing_sent_piece]  7.19 us
  transfers between devices with their start and end apart: 5, of which 3 were waited for; matrix products, arithmetic and copies ran while one was open for 19% of the time, Pallas kernels for 0%

commit v1 on v0

--- a/solution.py
+++ b/solution.py
@@ -49,7 +49,9 @@
     waves = fetch_list.shape[0]
     own_unit = normalize(embeds)
     own_pieces = own_unit.reshape(owned, pieces, slice_rows, width)
-    owned_full = lax.all_gather(own_unit, "gy", axis=1, tiled=True)
+    owned_full = jnp.concatenate(
+        lax.all_to_all(jnp.stack([own_unit] * lax.axis_size("gy")), "gy", 0, 0), axis=1
+    )
     positions = jnp.arange(block, dtype=jnp.int32)
     own_counts = lax.dynamic_slice_in_dim(counts, first, owned)
     col_valid = positions[None, :] < own_counts[:, None]

time: 225 us -> 280 us (1.24)
  waiting for transfers between devices: 102 us -> 153 us
  local copies, waits for them, and re-layouts: 11.2 us -> 27.5 us
  between operations: 13.7 us -> 0.29 us
  starting transfers between devices: 44 us -> 47.8 us
    all_to_all x0 -> x1, waiting for transfers between devices: none -> 125 us  [on_device(): lax.all_to_all(jnp.stack([own_unit] * lax.axis_size('gy')), 'gy', 0, 0)]
    all_gather x1 -> x0, waiting for transfers between devices: 76.8 us -> none  [on_device(): owned_full = lax.all_gather(own_unit, 'gy', axis=1, tiled=True)]
    all_to_all x0 -> x1, local copies, waits for them, and re-layouts: none -> 10.7 us  [on_device(): lax.all_to_all(jnp.stack([own_unit] * lax.axis_size('gy')), 'gy', 0, 0)]
    all_to_all x0 -> x1, starting transfers between devices: none -> 6.61 us  [on_device(): lax.all_to_all(jnp.stack([own_unit] * lax.axis_size('gy')), 'gy', 0, 0)]
    another operation x2 -> x3, local copies, waits for them, and re-layouts: 0.02 us -> 5.81 us  [the longest x1 5.79 us: on_device(): jnp.stack([own_unit] * lax.axis_size('gy'))]
    all_to_all x2, starting transfers between devices: 24.9 us -> 19.9 us  [on_device(): lax.all_to_all(row_best, 'gx', split_axis=0, concat_axis=0, tiled=True)]
  transfers between devices with their start and end apart: 5 -> 5, of which waited for: 3 -> 4; matrix products, arithmetic and copies ran while one was open for 19% -> 19% of each run, Pallas kernels for 0% -> 0%
where the time goes in v1:
time: 280 us; the launch traced here: 279 us
  waiting for transfers between devices  153 us (55%)
  starting transfers between devices  47.8 us (17%)
  local copies, waits for them, and re-layouts  27.5 us (10%)
  matrix products  24.9 us (9%)
  other arithmetic  13.7 us (5%)
  blocking collectives  11.8 us (4%)
    all_to_all x1, waiting for transfers between devices, on_device(): lax.all_to_all(jnp.stack([own_unit] * lax.axis_size('gy')), 'gy', 0, 0)  125 us
    dot_general x4, matrix products, advance(): jnp.einsum('rd,cbd->rcb', flat_rows, columns, preferred_element_type=jnp....  24.9 us
    all_to_all x2, starting transfers between devices, on_device(): lax.all_to_all(outbound, 'gx', split_axis=0, concat_axis=0, tiled=True)  21.2 us
    all_to_all x2, starting transfers between devices, on_device(): lax.all_to_all(row_best, 'gx', split_axis=0, concat_axis=0, tiled=True)  19.9 us
    all_to_all x2, waiting for transfers between devices, on_device(): lax.all_to_all(outbound, 'gx', split_axis=0, concat_axis=0, tiled=True)  19.2 us
    pmax x1, blocking collectives, on_device(): col_all = lax.pmax(col_total, 'gy')  11.8 us
    all_to_all x1, local copies, waits for them, and re-layouts, on_device(): lax.all_to_all(jnp.stack([own_unit] * lax.axis_size('gy')), 'gy', 0, 0)  10.7 us
    all_to_all x2, waiting for transfers between devices, on_device(): lax.all_to_all(row_best, 'gx', split_axis=0, concat_axis=0, tiled=True)  9.18 us
  transfers between devices with their start and end apart: 5, of which 4 were waited for; matrix products, arithmetic and copies ran while one was open for 19% of the time, Pallas kernels for 0%

profile of v1, /device:TPU:1, one launch (start us, length us, event | category | flops | bytes accessed | tf_op | source)
XLA Modules:
  0.0 279.5 jit_solution(2758956721859116921)
XLA Ops:
  0.0 2.6 fusion.18
  2.6 2.5 fusion.19
  5.1 5.8 %stack.2 = bf16[4,4,512,768]{3,2,1,0:T(8,128)(2,1)} broadcast(bf16[4,512,768]{2,1,0:T(8,128)(2,1)S(1)} %fusion.19), dimensions={1,2,3} | broadcast | bytes 15728640 | tf_op jit(solution)/shard_map/stack | solution.py:53
  10.9 6.6 %all-to-all-start = ((bf16[4,4,512,768]{3,2,1,0:T(8,128)(2,1)}), bf16[4,4,512,768]{3,2,1,0:T(8,128)(2,1)}, u32[]{:S(2)}, u32[]{:S(2)}) async-start(bf16[4,4,512,768]{3,2,1,0:T(8,128)(2,1)} %stack.2), calls=%async_computation | async-start | bytes 25165824 | tf_op jit(solution)/shard_map/all_to_all | solution.py:53
  17.6 0.1 dynamic_slice.48
  17.7 0.1 lt.161
  17.8 0.8 gather_fusion.2
  18.7 0.2 dynamic-slice_reduce_fusion
  18.9 2.3 fusion.48
  21.2 3.5 %gather_fusion.3 = bf16[64,8,768]{2,1,0:T(8,128)(2,1)} fusion(bf16[4,64,8,768]{3,2,1,0:T(8,128)(2,1)} %fusion.48, s32[64]{0:T(128)S(1)} %fusion.42), kind=kCustom, calls=%fused_computation.3 | custom fusion | bytes 1573376 | tf_op jit(solution)/shard_map/gather | solution.py:68
  24.7 0.2 dynamic-slice_reduce_fusion.1
  24.9 3.5 %gather_fusion.1 = bf16[64,8,768]{2,1,0:T(8,128)(2,1)} fusion(bf16[4,64,8,768]{3,2,1,0:T(8,128)(2,1)} %fusion.48, s32[64]{0:T(128)S(1)} %fusion.43), kind=kCustom, calls=%fused_computation.1 | custom fusion | bytes 1573376 | tf_op jit(solution)/shard_map/gather | solution.py:68
  28.4 0.8 gather_fusion
  29.3 0.1 iota_compare_fusion
  29.3 125.0 %all-to-all-done = bf16[4,4,512,768]{3,2,1,0:T(8,128)(2,1)} async-done(((bf16[4,4,512,768]{3,2,1,0:T(8,128)(2,1)}), bf16[4,4,512,768]{3,2,1,0:T(8,128)(2,1)}, u32[]{:S(2)}, u32[]{:S(2)}) %all-to-all-start) | async-done | bytes 12582944 | tf_op jit(solution)/shard_map/all_to_all | solution.py:53
  154.4 15.3 %all-to-all-start.3 = ((bf16[64,8,768]{2,1,0:T(8,128)(2,1)}), bf16[64,8,768]{2,1,0:T(8,128)(2,1)S(1)}, u32[]{:S(2)}, u32[]{:S(2)}) async-start(bf16[64,8,768]{2,1,0:T(8,128)(2,1)} %gather_fusion.3), calls=%async_computation.3 | async-start | bytes 1572864 | tf_op jit(solution)/shard_map/all_to_all | solution.py:69
  169.7 0.1 iota_compare_fusion.1
  169.8 0.1 iota_compare_fusion.4
  169.9 0.1 broadcast_and_fusion.2
  170.0 0.1 broadcast_and_fusion.3
  170.2 0.1 iota_compare_fusion.2
  170.3 10.7 %copy.16 = bf16[4,4,512,768]{3,2,0,1:T(8,128)(2,1)} copy(bf16[4,4,512,768]{3,2,1,0:T(8,128)(2,1)} %all-to-all-done) | data formatting | bytes 25165824 | tf_op jit(solution)/shard_map/all_to_all | solution.py:53
  181.0 11.7 %all-to-all-done.3 = bf16[64,8,768]{2,1,0:T(8,128)(2,1)S(1)} async-done(((bf16[64,8,768]{2,1,0:T(8,128)(2,1)}), bf16[64,8,768]{2,1,0:T(8,128)(2,1)S(1)}, u32[]{:S(2)}, u32[]{:S(2)}) %all-to-all-start.3) | async-done | bytes 786464 | tf_op jit(solution)/shard_map/all_to_all | solution.py:69
  192.7 5.9 %all-to-all-start.1 = ((bf16[64,8,768]{2,1,0:T(8,128)(2,1)}), bf16[64,8,768]{2,1,0:T(8,128)(2,1)S(1)}, u32[]{:S(2)}, u32[]{:S(2)}) async-start(bf16[64,8,768]{2,1,0:T(8,128)(2,1)} %gather_fusion.1), calls=%async_computation.1 | async-start | bytes 1572864 | tf_op jit(solution)/shard_map/all_to_all | solution.py:69
  198.6 15.5 %while.27 = (s32[]{:T(128)}, f32[64,8]{1,0:T(8,128)}, f32[2,2,2048]{2,1,0:T(2,128)S(1)}, pred[2,64,2]{1,2,0:T(4,128)(4,1)S(1)}, pred[2,2,2048]{2,1,0:T(4,128)(4,...) while((s32[]{:T(128)}, f32[64,8]{1,0:T(8,128)}, ...), condition=%wide.region_11.12_spmd.clone, body=%wide.region_8.11_spmd.clone.sunk | while | flops 3229612544 | bytes 7160887 | solution.py:37
  198.7 0.1 and.439
  198.7 0.1 and.440
  198.9 0.1 add_compare_fusion.5
  198.9 0.1 and.441
  199.1 6.2 %fusion.52 = (f32[2,2048]{1,0:T(2,128)S(1)}, f32[512]{0:T(512)S(1)}) fusion(pred[2,2048]{1,0:T(4,128)(4,1)S(1)} %dynamic-slice_bitcast_fusion.10, pred[512,2]{0,1:T(4,128)(4,1)S(1)} %broadcast_and_fusion.7, bf16[512,768]{1,0:T(8,128)(2,1)S(1)} %get-tuple-element.389, bf16[2,2,2048,768]{3,2,1,0:T(8,128)(2,1)} %get-tuple-element.388, s32[]{:T(128)S(6)} %copy.23), kind=kOutput, calls=%fused_computation.21.clone.1 | convolution fusion | flops 3229609472 | bytes 7101444 | tf_op jit(solution)/shard_map/while/body/eval_jaxpr/rd,cbd->rcb/dot_general | solution.py:30
  205.3 0.1 reduce_max.79
  205.4 0.6 select_maximum_fusion.5
  206.0 0.1 and.439
  206.1 0.1 and.440
  206.2 0.1 add_compare_fusion.5
  206.3 0.1 and.441
  206.4 6.2 %fusion.52 = (f32[2,2048]{1,0:T(2,128)S(1)}, f32[512]{0:T(512)S(1)}) fusion(pred[2,2048]{1,0:T(4,128)(4,1)S(1)} %dynamic-slice_bitcast_fusion.10, pred[512,2]{0,1:T(4,128)(4,1)S(1)} %broadcast_and_fusion.7, bf16[512,768]{1,0:T(8,128)(2,1)S(1)} %get-tuple-element.389, bf16[2,2,2048,768]{3,2,1,0:T(8,128)(2,1)} %get-tuple-element.388, s32[]{:T(128)S(6)} %copy.23), kind=kOutput, calls=%fused_computation.21.clone.1 | convolution fusion | flops 3229609472 | bytes 7101444 | tf_op jit(solution)/shard_map/while/body/eval_jaxpr/rd,cbd->rcb/dot_general | solution.py:30
  212.7 0.1 reduce_max.79
  212.8 1.4 select_maximum_fusion.5
  214.1 7.4 %all-to-all-done.1 = bf16[64,8,768]{2,1,0:T(8,128)(2,1)S(1)} async-done(((bf16[64,8,768]{2,1,0:T(8,128)(2,1)}), bf16[64,8,768]{2,1,0:T(8,128)(2,1)S(1)}, u32[]{:S(2)}, u32[]{:S(2)}) %all-to-all-start.1) | async-done | bytes 786464 | tf_op jit(solution)/shard_map/all_to_all | solution.py:69
  221.6 5.9 %all-to-all-start.4 = ((f32[64,1,8]{2,1,0:T(1,128)}), f32[64,1,8]{2,1,0:T(1,128)S(1)}, u32[]{:S(2)}, u32[]{:S(2)}) async-start(f32[64,1,8]{2,1,0:T(1,128)} %bitcast.20), calls=%async_computation.4 | async-start | bytes 65536 | tf_op jit(solution)/shard_map/all_to_all | solution.py:76
  227.5 15.5 %while.26 = (s32[]{:T(128)}, f32[64,8]{1,0:T(8,128)}, f32[2,2,2048]{2,1,0:T(2,128)S(1)}, pred[2,64,2]{1,2,0:T(4,128)(4,1)S(1)}, pred[2,2,2048]{2,1,0:T(4,128)(4,...) while((s32[]{:T(128)}, f32[64,8]{1,0:T(8,128)}, ...), condition=%wide.region_5.6_spmd.clone, body=%wide.region_2.5_spmd.clone.sunk | while | flops 3229612544 | bytes 7160887 | solution.py:37
  227.6 0.1 and.431
  227.7 0.1 and.432
  227.8 0.1 add_compare_fusion.4
  227.9 0.1 and.433
  228.0 6.2 %fusion.51 = (f32[2,2048]{1,0:T(2,128)S(1)}, f32[512]{0:T(512)S(1)}) fusion(pred[2,2048]{1,0:T(4,128)(4,1)S(1)} %dynamic-slice_bitcast_fusion.8, pred[512,2]{0,1:T(4,128)(4,1)S(1)} %broadcast_and_fusion.6, bf16[512,768]{1,0:T(8,128)(2,1)S(1)} %get-tuple-element.425, bf16[2,2,2048,768]{3,2,1,0:T(8,128)(2,1)} %get-tuple-element.424, s32[]{:T(128)S(6)} %copy.32), kind=kOutput, calls=%fused_computation.7.clone.1 | convolution fusion | flops 3229609472 | bytes 7101444 | tf_op jit(solution)/shard_map/while/body/eval_jaxpr/rd,cbd->rcb/dot_general | solution.py:30
  234.2 0.1 reduce_max.77
  234.3 0.6 select_maximum_fusion.4
  235.0 0.1 and.431
  235.0 0.1 and.432
  235.2 0.1 add_compare_fusion.4
  235.2 0.1 and.433
  235.4 6.2 %fusion.51 = (f32[2,2048]{1,0:T(2,128)S(1)}, f32[512]{0:T(512)S(1)}) fusion(pred[2,2048]{1,0:T(4,128)(4,1)S(1)} %dynamic-slice_bitcast_fusion.8, pred[512,2]{0,1:T(4,128)(4,1)S(1)} %broadcast_and_fusion.6, bf16[512,768]{1,0:T(8,128)(2,1)S(1)} %get-tuple-element.425, bf16[2,2,2048,768]{3,2,1,0:T(8,128)(2,1)} %get-tuple-element.424, s32[]{:T(128)S(6)} %copy.32), kind=kOutput, calls=%fused_computation.7.clone.1 | convolution fusion | flops 3229609472 | bytes 7101444 | tf_op jit(solution)/shard_map/while/body/eval_jaxpr/rd,cbd->rcb/dot_general | solution.py:30
  241.6 0.1 reduce_max.77
  241.7 1.4 select_maximum_fusion.4
  243.1 11.8 %pmax.7 = f32[4,2048]{1,0:T(4,128)S(1)} all-reduce(f32[4,2048]{1,0:T(4,128)S(1)} %max.26), channel_id=1, replica_groups=mesh['gx'=64,'gy'=4] {'gy'}, use_global_device_ids=true, to_apply=%region_13.14 | all-reduce | flops 8192 | bytes 65536 | tf_op jit(solution)/shard_map/pmax | solution.py:85
  254.9 14.0 %all-to-all-start.2 = ((f32[64,1,8]{2,1,0:T(1,128)}), f32[64,1,8]{2,1,0:T(1,128)S(1)}, u32[]{:S(2)}, u32[]{:S(2)}) async-start(f32[64,1,8]{2,1,0:T(1,128)} %bitcast.10), calls=%async_computation.2 | async-start | bytes 65536 | tf_op jit(solution)/shard_map/all_to_all | solution.py:76
  268.9 0.2 select_reduce_fusion
  269.2 9.2 %all-to-all-done.2 = f32[64,1,8]{2,1,0:T(1,128)S(1)} async-done(((f32[64,1,8]{2,1,0:T(1,128)}), f32[64,1,8]{2,1,0:T(1,128)S(1)}, u32[]{:S(2)}, u32[]{:S(2)}) %all-to-all-start.2) | async-done | bytes 2080 | tf_op jit(solution)/shard_map/all_to_all | solution.py:76
  278.3 0.2 select_reduce_fusion.1
  278.6 0.1 copy.17
  278.7 0.1 max.24
  278.8 0.7 maximum_select_fusion
  (51 shorter events, 0.6 us)
Async XLA Ops:
  10.9 6.7 %copy-start.2 = (s32[2,64,64,2]{2,3,1,0:T(2,128)S(1)}, s32[2,64,64,2]{2,3,1,0:T(2,128)}, u32[]{:S(2)}) copy-start(s32[2,64,64,2]{2,3,1,0:T(2,128)} %param.10) | copy-start | bytes 196612
  10.9 6.7 %copy-start = (s32[256]{0:T(256)S(1)}, s32[256]{0:T(256)}, u32[]{:S(2)}) copy-start(s32[256]{0:T(256)} %param.11) | copy-start | bytes 3076
  10.9 6.9 %copy-start.3 = (s32[2,64,64]{2,1,0:T(8,128)S(1)}, s32[2,64,64]{2,1,0:T(8,128)}, u32[]{:S(2)}) copy-start(s32[2,64,64]{2,1,0:T(8,128)} %param.9) | copy-start | bytes 98308
  10.9 8.0 %copy-start.1 = (bf16[4,512,768]{2,1,0:T(8,128)(2,1)S(1)}, bf16[4,512,768]{2,1,0:T(8,128)(2,1)}, u32[]{:S(2)}) copy-start(bf16[4,512,768]{2,1,0:T(8,128)(2,1)} %param.8) | copy-start | bytes 9437188
  10.9 143.5 %all-to-all-start = ((bf16[4,4,512,768]{3,2,1,0:T(8,128)(2,1)}), bf16[4,4,512,768]{3,2,1,0:T(8,128)(2,1)}, u32[]{:S(2)}, u32[]{:S(2)}) async-start(bf16[4,4,512,768]{3,2,1,0:T(8,128)(2,1)} %stack.2), calls=%async_computation | async-start | bytes 25165824 | tf_op jit(solution)/shard_map/all_to_all | solution.py:53
  154.4 38.3 %all-to-all-start.3 = ((bf16[64,8,768]{2,1,0:T(8,128)(2,1)}), bf16[64,8,768]{2,1,0:T(8,128)(2,1)S(1)}, u32[]{:S(2)}, u32[]{:S(2)}) async-start(bf16[64,8,768]{2,1,0:T(8,128)(2,1)} %gather_fusion.3), calls=%async_computation.3 | async-start | bytes 1572864 | tf_op jit(solution)/shard_map/all_to_all | solution.py:69
  192.7 28.9 %all-to-all-start.1 = ((bf16[64,8,768]{2,1,0:T(8,128)(2,1)}), bf16[64,8,768]{2,1,0:T(8,128)(2,1)S(1)}, u32[]{:S(2)}, u32[]{:S(2)}) async-start(bf16[64,8,768]{2,1,0:T(8,128)(2,1)} %gather_fusion.1), calls=%async_computation.1 | async-start | bytes 1572864 | tf_op jit(solution)/shard_map/all_to_all | solution.py:69
  221.6 33.3 %all-to-all-start.4 = ((f32[64,1,8]{2,1,0:T(1,128)}), f32[64,1,8]{2,1,0:T(1,128)S(1)}, u32[]{:S(2)}, u32[]{:S(2)}) async-start(f32[64,1,8]{2,1,0:T(1,128)} %bitcast.20), calls=%async_computation.4 | async-start | bytes 65536 | tf_op jit(solution)/shard_map/all_to_all | solution.py:76
  254.9 23.5 %all-to-all-start.2 = ((f32[64,1,8]{2,1,0:T(1,128)}), f32[64,1,8]{2,1,0:T(1,128)S(1)}, u32[]{:S(2)}, u32[]{:S(2)}) async-start(f32[64,1,8]{2,1,0:T(1,128)} %bitcast.10), calls=%async_computation.2 | async-start | bytes 65536 | tf_op jit(solution)/shard_map/all_to_all | solution.py:76
